TPU v7x, 512 devices: a whole 4x4x16 slice. The times are simulated.
512 devices in a mesh: graph: 32 (over z, core), irreps: 16 (over y, x).
Axes of the slice: x: 4, y: 4, z: 16, core: 2. Of those that a mesh axis runs over, the one named last changes fastest.
Arguments:
- node_feats: bfloat16 [49, 128, 2048], P(None, 'irreps', 'graph'), may hold values from -8 to 8
- norm_gain: float32 [7, 128], P(None, 'irreps'), may hold values from 0.1 to 1.9
- species: int32 [2048], P('graph'), may hold values from 0 to 89
- send_list: int32 [8192], P('graph'), may hold values from 0 to 63
- edge_source: int32 [32768], P('graph'), may hold values from 0 to 319, as said below
- edge_target: int32 [32768], P('graph'), may hold values from 0 to 63
- edge_count: int32 [32], P('graph'), may hold values from 512 to 1024, as said below
- edge_length: float32 [32768], P('graph'), may hold values from 0.8 to 6
- wigner: bfloat16 [235, 32768], P(None, 'graph'), may hold values from -2.5 to 2.5
- radial_in: bfloat16 [512, 128], replicated, may hold values from -0.25 to 0.25
- species_table: bfloat16 [90, 128], replicated, may hold values from -6 to 6
- radial_out: bfloat16 [128, 896], replicated, may hold values from -0.5 to 0.5
- order_zero: bfloat16 [896, 896], replicated, may hold values from -0.1875 to 0.1875
- order_one: bfloat16 [2, 768, 768], replicated, may hold values from -0.15625 to 0.15625
- order_two: bfloat16 [2, 640, 640], replicated, may hold values from -0.15625 to 0.15625
- project_weight: bfloat16 [7, 128, 128], P(None, None, 'irreps'), may hold values from -0.5 to 0.5
Outputs:
- new_feats: bfloat16 [49, 128, 2048], P(None, 'irreps', 'graph')
Inputs may be any that keep to these rules, and one draw needn't show every extreme that they name: `edge_source`: an index into the table of its edge's domain. A domain reads no slot of its own send block; from each other domain it reads only the first few slots (between 1 and 8 of them), and it reads slot 7 of some domain. `edge_count`: edge slots at or past a domain's count are padding; some domain has all 1024 live.
All inputs are finite; a program needn't handle non-finite values.
Results may differ from a plain program's by a relative error of at most 0.006.
Values may be sent and summed in bfloat16 or wider, within the bound.
No kernel may reach another device: no remote copies, remote signals or barrier semaphores. Data moves between devices by JAX's collectives and lax.ppermute only.
A program may use at most 128 MiB of HBM per device.

v0:
```python
import jax
import jax.numpy as jnp
import numpy as np
from jax import lax
from jax.sharding import PartitionSpec as P

CHANNELS = 128
MAX_DEGREE = 6
MAX_ORDER = 2
ROTATED = 29
EPSILON = 1e-06
CUTOFF = 6.0


def order_index(degree, harmonic):
    if harmonic == 0:
        return degree
    first_row = MAX_DEGREE + 1
    for level in range(1, abs(harmonic)):
        first_row = first_row + 2 * (MAX_DEGREE + 1 - level)
    if harmonic < 0:
        first_row = first_row + MAX_DEGREE + 1 - abs(harmonic)
    return first_row + degree - abs(harmonic)


def wigner_start(degree):
    running = 0
    for level in range(degree):
        running = running + (2 * min(level, MAX_ORDER) + 1) * (2 * level + 1)
    return running


def left_dot(weight, values):
    return lax.dot_general(
        weight, values, (((0,), (0,)), ((), ())), preferred_element_type=jnp.float32
    )


def degree_sums(squares):
    return jnp.stack(
        [
            jnp.sum(squares[degree * degree : (degree + 1) ** 2], axis=0)
            for degree in range(MAX_DEGREE + 1)
        ]
    )


def normalize(node_feats, norm_gain, totals):
    levels = MAX_DEGREE + 1
    degree_of = np.repeat(np.arange(levels), 2 * np.arange(levels) + 1)
    entry_counts = (2 * np.arange(levels) + 1) * CHANNELS
    inverse = 1.0 / jnp.sqrt(totals / jnp.asarray(entry_counts, jnp.float32)[:, None] + EPSILON)
    gain_rows = norm_gain[degree_of]
    scale_rows = inverse[degree_of]
    return (node_feats.astype(jnp.float32) * gain_rows[:, :, None] * scale_rows[:, None, :]).astype(
        jnp.bfloat16
    )


def normalize_rows(values, gain_full, totals):
    levels = MAX_DEGREE + 1
    degree_of = np.repeat(np.arange(levels), 2 * np.arange(levels) + 1)
    entry_counts = (2 * np.arange(levels) + 1) * CHANNELS
    inverse = 1.0 / jnp.sqrt(totals / jnp.asarray(entry_counts, jnp.float32)[:, None] + EPSILON)
    gain_rows = gain_full[degree_of]
    scale_rows = inverse[degree_of]
    return (values * gain_rows[:, :, None] * scale_rows[:, None, :]).astype(jnp.bfloat16)


def rotate(source, wig_rows):
    pieces = [None] * ROTATED
    for degree in range(MAX_DEGREE + 1):
        reach_order = min(degree, MAX_ORDER)
        span_cols = 2 * degree + 1
        first_row = wigner_start(degree)
        for position in range(2 * reach_order + 1):
            total = None
            for column in range(span_cols):
                term = (
                    wig_rows[first_row + position * span_cols + column][None, :]
                    * source[degree * degree + column]
                )
                total = term if total is None else total + term
            pieces[order_index(degree, position - reach_order)] = total
    return jnp.stack(pieces).astype(jnp.bfloat16)


def unrotate(gated, wig_rows):
    pieces = []
    for degree in range(MAX_DEGREE + 1):
        reach_order = min(degree, MAX_ORDER)
        span_cols = 2 * degree + 1
        first_row = wigner_start(degree)
        for column in range(span_cols):
            total = None
            for position in range(2 * reach_order + 1):
                term = (
                    wig_rows[first_row + position * span_cols + column][None, :]
                    * gated[order_index(degree, position - reach_order)]
                )
                total = term if total is None else total + term
            pieces.append(total)
    return jnp.stack(pieces)


def radial_weights(lengths, kind_ids, radial_in, species_table, radial_out):
    basis_count = radial_in.shape[0]
    spacing = CUTOFF / (basis_count - 1)
    centers = jnp.arange(basis_count, dtype=jnp.float32) * spacing
    basis_rows = jnp.exp(
        -0.5 * jnp.square((lengths[None, :] - centers[:, None]) / (2.0 * spacing))
    ).astype(jnp.bfloat16)
    onehot = (
        kind_ids[None, :] == jnp.arange(species_table.shape[0], dtype=jnp.int32)[:, None]
    ).astype(jnp.bfloat16)
    hidden = jax.nn.silu(left_dot(radial_in, basis_rows) + left_dot(species_table, onehot)).astype(
        jnp.bfloat16
    )
    return left_dot(radial_out, hidden)


def convolve(rotated, radial, order_zero, order_one, order_two):
    levels = MAX_DEGREE + 1
    channel_count = rotated.shape[1]
    num_edges = rotated.shape[2]
    lowest = (
        rotated[:levels].astype(jnp.float32).reshape(levels * channel_count, num_edges) * radial
    ).astype(jnp.bfloat16)
    outputs = [left_dot(order_zero, lowest).reshape(levels, channel_count, num_edges)]
    first_row = levels
    for harmonic, weight in ((1, order_one), (2, order_two)):
        span_rows = levels - harmonic
        plus_rows = rotated[first_row : first_row + span_rows].reshape(
            span_rows * channel_count, num_edges
        )
        minus_rows = rotated[first_row + span_rows : first_row + 2 * span_rows].reshape(
            span_rows * channel_count, num_edges
        )
        joined = jnp.concatenate([plus_rows, minus_rows], axis=1)
        real_part = left_dot(weight[0], joined)
        cross_part = left_dot(weight[1], joined)
        outputs.append(
            (real_part[:, :num_edges] - cross_part[:, num_edges:]).reshape(
                span_rows, channel_count, num_edges
            )
        )
        outputs.append(
            (cross_part[:, :num_edges] + real_part[:, num_edges:]).reshape(
                span_rows, channel_count, num_edges
            )
        )
        first_row = first_row + 2 * span_rows
    mixed = jnp.concatenate(outputs, axis=0)
    scalar = mixed[0]
    return jnp.concatenate(
        [jax.nn.silu(scalar)[None], mixed[1:] * jax.nn.sigmoid(scalar)[None]], axis=0
    ).astype(jnp.bfloat16)


def split_dot(values, weight):
    upper_part = values.astype(jnp.bfloat16)
    lower_part = (values - upper_part.astype(jnp.float32)).astype(jnp.bfloat16)
    return jnp.dot(upper_part, weight, preferred_element_type=jnp.float32) + jnp.dot(
        lower_part, weight, preferred_element_type=jnp.float32
    )


def body(
    node_feats,
    norm_gain,
    species,
    send_list,
    edge_source,
    edge_target,
    edge_count,
    edge_length,
    wigner,
    radial_in,
    species_table,
    radial_out,
    order_zero,
    order_one,
    order_two,
    project_weight,
):
    levels = MAX_DEGREE + 1
    owners = lax.axis_size("irreps")
    quarter = lax.axis_index("irreps")
    coeffs, span_chan, atom_count = node_feats.shape
    per_owner = edge_source.shape[0] // owners
    first_edge = quarter * per_owner
    outgoing = node_feats[:, :, send_list]
    arrived = lax.all_to_all(outgoing, "graph", split_axis=2, concat_axis=2, tiled=True)
    packed = jnp.concatenate(
        [norm_gain, project_weight.astype(jnp.float32).reshape(levels, -1)], axis=1
    )
    spread = lax.all_to_all(
        jnp.broadcast_to(packed[None], (owners,) + packed.shape), "irreps", 0, 0, tiled=True
    )
    gain_full = jnp.transpose(spread[:, :, :span_chan], (1, 0, 2)).reshape(
        levels, owners * span_chan
    )
    weight_full = jnp.transpose(
        spread[:, :, span_chan:].reshape(owners, levels, CHANNELS, span_chan), (1, 2, 0, 3)
    ).reshape(levels, CHANNELS, owners * span_chan)
    lookup = jnp.concatenate([node_feats, arrived], axis=2)
    source = lax.all_to_all(
        lookup[:, :, edge_source], "irreps", split_axis=2, concat_axis=1, tiled=True
    )
    source = source.astype(jnp.float32)
    squares = jnp.sum(jnp.square(source), axis=1)
    totals = degree_sums(squares)
    normed = normalize_rows(source, gain_full, totals)
    wig_mine = lax.dynamic_slice_in_dim(wigner, first_edge, per_owner, 1).astype(jnp.float32)
    rotated = rotate(normed.astype(jnp.float32), wig_mine)
    targets_mine = lax.dynamic_slice_in_dim(edge_target, first_edge, per_owner)
    lengths_mine = lax.dynamic_slice_in_dim(edge_length, first_edge, per_owner)
    radial = radial_weights(
        lengths_mine, species[targets_mine], radial_in, species_table, radial_out
    )
    gated = convolve(rotated, radial, order_zero, order_one, order_two)
    messages = unrotate(gated.astype(jnp.float32), wig_mine)
    edge_weight = jnp.where(
        first_edge + jnp.arange(per_owner, dtype=jnp.int32) < edge_count[0], 0.25, 0.0
    ).astype(jnp.float32)
    onehot = jnp.where(
        targets_mine[:, None] == jnp.arange(atom_count, dtype=jnp.int32)[None, :],
        edge_weight[:, None],
        0.0,
    ).astype(jnp.bfloat16)
    summed = split_dot(messages.reshape(-1, per_owner), onehot).reshape(
        coeffs, CHANNELS, atom_count
    )
    upper_part = summed.astype(jnp.bfloat16)
    lower_part = (summed - upper_part.astype(jnp.float32)).astype(jnp.bfloat16)
    updates = []
    for degree in range(levels):
        rows = slice(degree * degree, (degree + 1) ** 2)
        weight = weight_full[degree].astype(jnp.bfloat16)
        updates.append(
            jnp.einsum("io,jia->oja", weight, upper_part[rows], preferred_element_type=jnp.float32)
            + jnp.einsum(
                "io,jia->oja", weight, lower_part[rows], preferred_element_type=jnp.float32
            )
        )
    projected = jnp.concatenate(updates, axis=1)
    returned = lax.all_to_all(
        projected.reshape(owners, span_chan, coeffs, atom_count), "irreps", 0, 0, tiled=True
    )
    total = jnp.transpose(jnp.sum(returned, axis=0), (1, 0, 2))
    return (node_feats.astype(jnp.float32) + total).astype(jnp.bfloat16)


def solution(mesh):
    return jax.shard_map(
        body,
        mesh=mesh,
        in_specs=(
            P(None, "irreps", "graph"),
            P(None, "irreps"),
            P("graph"),
            P("graph"),
            P("graph"),
            P("graph"),
            P("graph"),
            P("graph"),
            P(None, "graph"),
            P(),
            P(),
            P(),
            P(),
            P(),
            P(),
            P(None, None, "irreps"),
        ),
        out_specs=P(None, "irreps", "graph"),
        check_vma=False,
    )
```

profile of v0, /device:TPU:2, one launch (start us, length us, event | category | flops | bytes accessed | tf_op | source)
XLA Modules:
  0.0 238.1 jit_solution(476793149073174638)
XLA Ops:
  0.0 1.2 copy.225
  3.4 2.0 reshape.3035
  5.5 15.5 %all-to-all-start.1 = ((bf16[32,2,1568]{2,1,0:T(2,128)(2,1)}), bf16[32,2,1568]{2,1,0:T(2,128)(2,1)S(1)}, u32[]{:S(2)}, u32[]{:S(2)}) async-start(bf16[32,2,1568]{2,1,0:T(2,128)(2,1)} %reshape.3035), calls=%async_computation.1 | async-start | bytes 425984 | tf_op jit(solution)/shard_map/all_to_all | solution.py:193
  21.0 0.9 dynamic-slice_convert_fusion
  30.8 1.3 compare_select_fusion.2
  34.0 7.6 %all-to-all-done.1 = bf16[32,2,1568]{2,1,0:T(2,128)(2,1)S(1)} async-done(((bf16[32,2,1568]{2,1,0:T(2,128)(2,1)}), bf16[32,2,1568]{2,1,0:T(2,128)(2,1)S(1)}, u32[]{:S(2)}, u32[]{:S(2)}) %all-to-all-start.1) | async-done | bytes 200736 | tf_op jit(solution)/shard_map/all_to_all | solution.py:193
  41.6 0.9 broadcast_in_dim.56
  42.6 7.5 %all-to-all-start = ((f32[16,7,1032]{2,1,0:T(8,128)}), f32[16,7,1032]{2,1,0:T(8,128)}, u32[]{:S(2)}, u32[]{:S(2)}) async-start(f32[16,7,1032]{2,1,0:T(8,128)} %broadcast_in_dim.56), calls=%async_computation | async-start | bytes 1179648 | tf_op jit(solution)/shard_map/all_to_all | solution.py:197
  50.0 1.6 reshape.3036
  51.8 7.7 %gather_fusion.1 = bf16[1024,49,8]{1,2,0:T(8,128)(2,1)} fusion(bf16[49,8,320]{0,1,2:T(8,128)(2,1)S(1)} %pad_maximum_fusion, s32[1024]{0:T(1024)S(1)} %get-tuple-element.263), kind=kCustom, calls=%fused_computation.1 | custom fusion | bytes 1609728 | tf_op jit(solution)/shard_map/gather | solution.py:208
  59.5 3.1 %bitcast_bitcast_fusion = bf16[1024,8,49]{2,1,0:T(8,128)(2,1)} fusion(bf16[1024,49,8]{1,2,0:T(8,128)(2,1)} %gather_fusion.1), kind=kLoop, calls=%fused_computation.490 | loop fusion | bytes 1605632
  62.6 5.8 %reshape.3037 = bf16[16,2,12544]{2,1,0:T(2,128)(2,1)} reshape(bf16[1024,8,49]{2,1,0:T(8,128)(2,1)} %bitcast_bitcast_fusion) | data formatting | bytes 1605632
  68.4 7.4 %all-to-all-start.2 = ((bf16[16,2,12544]{2,1,0:T(2,128)(2,1)}), bf16[16,2,12544]{2,1,0:T(2,128)(2,1)S(1)}, u32[]{:S(2)}, u32[]{:S(2)}) async-start(bf16[16,2,12544]{2,1,0:T(2,128)(2,1)} %reshape.3037), calls=%async_computation.2 | async-start | bytes 1605632 | tf_op jit(solution)/shard_map/all_to_all | solution.py:207
  77.4 1.2 slice.2090
  78.7 1.6 copy.222
  80.4 2.4 %fusion.73 = (bf16[1,128,16,8]{2,3,1,0:T(8,128)(2,1)S(1)}, bf16[1,128,16,8]{2,3,1,0:T(8,128)(2,1)S(1)}, bf16[1,128,16,8]{2,3,1,0:T(8,128)(2,1)S(1)}, bf16[1,128,...) fusion(bf16[7,128,16,8]{2,3,1,0:T(8,128)(2,1)} %bitcast.748), kind=kLoop, calls=%fused_computation.487 | loop fusion | bytes 458752 | tf_op jit(solution)/shard_map/slice | solution.py:239
  82.8 1.8 copy.223
  85.5 1.8 copy.244
  87.3 1.8 copy.248
  92.8 7.4 %reshape.3038 = bf16[1024,8,49]{2,1,0:T(8,128)(2,1)} reshape(bf16[16,2,12544]{2,1,0:T(2,128)(2,1)S(1)} %all-to-all-done.2) | data formatting | bytes 1605632
  100.2 3.1 %multiply_reduce_fusion = f32[49,1024]{0,1:T(8,128)S(1)} fusion(bf16[1024,8,49]{2,1,0:T(8,128)(2,1)} %reshape.3038), kind=kLoop, calls=%fused_computation.6 | loop fusion | flops 1154048 | bytes 1003520 | tf_op jit(solution)/shard_map/reduce_sum | solution.py:211
  104.4 4.9 %copy.226 = f32[49,8,16,64]{3,1,2,0:T(8,128)} copy(bf16[49,8,16,64]{0,1,3,2:T(8,128)(2,1)} %bitcast.745) | data formatting | bytes 2408448 | tf_op jit(solution)/shard_map/convert_element_type | solution.py:210
  109.4 3.4 %copy.228 = f32[49,128,64]{1,2,0:T(8,128)} copy(f32[49,128,64]{2,1,0:T(8,128)} %bitcast.746) | data formatting | bytes 3211264 | tf_op jit(solution)/shard_map/convert_element_type | solution.py:210
  113.7 1.9 fusion.17
  119.7 0.9 constant_dynamic-update-slice_fusion.7
  120.7 1.6 constant_dynamic-update-slice_fusion.29
  122.3 1.4 constant_dynamic-update-slice_fusion.25
  123.7 1.4 constant_dynamic-update-slice_fusion.18
  127.3 0.9 constant_dynamic-update-slice_fusion.13
  128.4 1.1 convolution_bitcast_fusion.1
  129.7 1.1 convolution_bitcast_fusion
  131.1 0.9 constant_dynamic-update-slice_fusion.23
  132.9 0.9 constant_dynamic-update-slice_fusion.21
  134.5 0.9 constant_dynamic-update-slice_fusion.26
  136.0 1.1 convolution_bitcast_fusion.2
  139.6 1.4 constant_dynamic-update-slice_fusion
  141.0 1.5 fusion.9
  142.6 1.3 fusion.22
  187.8 1.2 copy.263
  189.9 1.6 bitcast_dynamic-update-slice_fusion.8
  194.0 0.9 bitcast_dynamic-update-slice_fusion.1
  194.9 1.0 bitcast_dynamic-update-slice_fusion
  195.8 2.1 copy.322
  198.0 3.0 %reshape.3039 = f32[16,1,25088]{2,1,0:T(1,128)} reshape(f32[16,49,8,64]{3,2,1,0:T(8,128)S(1)} %bitcast.747) | data formatting | bytes 3211264
  200.9 27.3 %all_to_all.24 = f32[16,1,25088]{2,1,0:T(1,128)S(1)} all-to-all(f32[16,1,25088]{2,1,0:T(1,128)} %reshape.3039), channel_id=1, replica_groups=mesh['graph'=32,'irreps'=16] {'irreps'}, dimensions={0} | all-to-all | bytes 3211264 | tf_op jit(solution)/shard_map/all_to_all | solution.py:247
  228.7 4.5 %reduce.4 = f32[16,25088]{1,0:T(8,128)S(1)} reduce(f32[16,1,25088]{2,1,0:T(1,128)S(1)} %all_to_all.24, f32[]{:T(128)} %broadcast.1939), dimensions={1}, to_apply=%all_to_all.19.reduce_sub_computation | reduce | bytes 3211268 | tf_op jit(solution)/shard_map/all_to_all | solution.py:247
  233.2 2.0 reshape.3040
  235.3 2.2 bitcast_reduce_fusion
  (741 shorter events, 76.5 us)
Async XLA Ops:
  0.0 141.0 %copy-start = (bf16[896,896]{1,0:T(8,128)(2,1)S(1)}, bf16[896,896]{1,0:T(8,128)(2,1)}, u32[]{:S(2)}) copy-start(bf16[896,896]{1,0:T(8,128)(2,1)} %param.32) | copy-start | bytes 4816900
  0.0 29.8 %copy-start.16 = (bf16[7,128,8]{1,2,0:T(8,128)(2,1)S(1)}, bf16[7,128,8]{1,2,0:T(8,128)(2,1)}, u32[]{:S(2)}) copy-start(bf16[7,128,8]{1,2,0:T(8,128)(2,1)} %param.35) | copy-start | bytes 43012
  3.4 29.5 %copy-start.274 = (s32[1024]{0:T(1024)S(1)}, s32[1024]{0:T(1024)}, u32[]{:S(2)}) copy-start(s32[1024]{0:T(1024)} %param.24) | copy-start | bytes 12292
  3.4 30.2 %copy-start.275 = (f32[7,8]{1,0:T(8,128)S(1)}, f32[7,8]{1,0:T(8,128)}, u32[]{:S(2)}) copy-start(f32[7,8]{1,0:T(8,128)} %param.21) | copy-start | bytes 676
  3.4 30.3 %copy-start.278 = (bf16[512,128]{1,0:T(8,128)(2,1)S(1)}, bf16[512,128]{1,0:T(8,128)(2,1)}, u32[]{:S(2)}) copy-start(bf16[512,128]{1,0:T(8,128)(2,1)} %param.29) | copy-start | bytes 393220
  5.5 36.2 %all-to-all-start.1 = ((bf16[32,2,1568]{2,1,0:T(2,128)(2,1)}), bf16[32,2,1568]{2,1,0:T(2,128)(2,1)S(1)}, u32[]{:S(2)}, u32[]{:S(2)}) async-start(bf16[32,2,1568]{2,1,0:T(2,128)(2,1)} %reshape.3035), calls=%async_computation.1 | async-start | bytes 425984 | tf_op jit(solution)/shard_map/all_to_all | solution.py:193
  25.2 108.9 %copy-start.23 = (f32[64]{0:T(128)}, f32[64]{0:T(128)S(1)}, u32[]{:S(2)}) copy-start(f32[64]{0:T(128)S(1)} %get-tuple-element.48) | copy-start | bytes 772
  25.2 108.9 %copy-start.25 = (f32[64]{0:T(128)}, f32[64]{0:T(128)S(1)}, u32[]{:S(2)}) copy-start(f32[64]{0:T(128)S(1)} %get-tuple-element.49) | copy-start | bytes 772
  42.6 25.9 %all-to-all-start = ((f32[16,7,1032]{2,1,0:T(8,128)}), f32[16,7,1032]{2,1,0:T(8,128)}, u32[]{:S(2)}, u32[]{:S(2)}) async-start(f32[16,7,1032]{2,1,0:T(8,128)} %broadcast_in_dim.56), calls=%async_computation | async-start | bytes 1179648 | tf_op jit(solution)/shard_map/all_to_all | solution.py:197
  62.6 13.8 %copy-start.2 = (s32[64]{0:T(128)S(1)}, s32[64]{0:T(128)}, u32[]{:S(2)}) copy-start(s32[64]{0:T(128)} %param.22) | copy-start | bytes 772
  68.4 24.4 %all-to-all-start.2 = ((bf16[16,2,12544]{2,1,0:T(2,128)(2,1)}), bf16[16,2,12544]{2,1,0:T(2,128)(2,1)S(1)}, u32[]{:S(2)}, u32[]{:S(2)}) async-start(bf16[16,2,12544]{2,1,0:T(2,128)(2,1)} %reshape.3037), calls=%async_computation.2 | async-start | bytes 1605632 | tf_op jit(solution)/shard_map/all_to_all | solution.py:207
  144.6 12.2 %copy-start.40 = (f32[64]{0:T(128)S(1)}, f32[64]{0:T(128)}, u32[]{:S(2)}) copy-start(f32[64]{0:T(128)} %get-tuple-element.104) | copy-start | bytes 772
  144.6 13.0 %copy-start.34 = (f32[64]{0:T(128)S(1)}, f32[64]{0:T(128)}, u32[]{:S(2)}) copy-start(f32[64]{0:T(128)} %get-tuple-element.105) | copy-start | bytes 772
  147.0 13.1 %copy-start.88 = (f32[64]{0:T(128)S(1)}, f32[64]{0:T(128)}, u32[]{:S(2)}) copy-start(f32[64]{0:T(128)} %get-tuple-element.56) | copy-start | bytes 772
  147.8 13.1 %copy-start.78 = (f32[64]{0:T(128)S(1)}, f32[64]{0:T(128)}, u32[]{:S(2)}) copy-start(f32[64]{0:T(128)} %get-tuple-element.55) | copy-start | bytes 772
  148.6 13.1 %copy-start.66 = (f32[64]{0:T(128)S(1)}, f32[64]{0:T(128)}, u32[]{:S(2)}) copy-start(f32[64]{0:T(128)} %get-tuple-element.54) | copy-start | bytes 772
  149.4 13.1 %copy-start.56 = (f32[64]{0:T(128)S(1)}, f32[64]{0:T(128)}, u32[]{:S(2)}) copy-start(f32[64]{0:T(128)} %get-tuple-element.53) | copy-start | bytes 772
  150.3 13.1 %copy-start.46 = (f32[64]{0:T(128)S(1)}, f32[64]{0:T(128)}, u32[]{:S(2)}) copy-start(f32[64]{0:T(128)} %get-tuple-element.52) | copy-start | bytes 772
  151.1 13.1 %copy-start.38 = (f32[64]{0:T(128)S(1)}, f32[64]{0:T(128)}, u32[]{:S(2)}) copy-start(f32[64]{0:T(128)} %get-tuple-element.47) | copy-start | bytes 772
  151.1 13.1 %copy-start.90 = (f32[64]{0:T(128)S(1)}, f32[64]{0:T(128)}, u32[]{:S(2)}) copy-start(f32[64]{0:T(128)} %get-tuple-element.230) | copy-start | bytes 772
  151.9 13.1 %copy-start.32 = (f32[64]{0:T(128)S(1)}, f32[64]{0:T(128)}, u32[]{:S(2)}) copy-start(f32[64]{0:T(128)} %get-tuple-element.51) | copy-start | bytes 772
  151.9 13.1 %copy-start.80 = (f32[64]{0:T(128)S(1)}, f32[64]{0:T(128)}, u32[]{:S(2)}) copy-start(f32[64]{0:T(128)} %get-tuple-element.237) | copy-start | bytes 772
  152.6 13.1 %copy-start.28 = (f32[64]{0:T(128)S(1)}, f32[64]{0:T(128)}, u32[]{:S(2)}) copy-start(f32[64]{0:T(128)} %get-tuple-element.50) | copy-start | bytes 772
  152.6 13.1 %copy-start.70 = (f32[64]{0:T(128)S(1)}, f32[64]{0:T(128)}, u32[]{:S(2)}) copy-start(f32[64]{0:T(128)} %get-tuple-element.236) | copy-start | bytes 772
  153.5 13.0 %copy-start.26 = (f32[64]{0:T(128)S(1)}, f32[64]{0:T(128)}, u32[]{:S(2)}) copy-start(f32[64]{0:T(128)} %copy-done.25) | copy-start | bytes 772
  153.5 13.0 %copy-start.60 = (f32[64]{0:T(128)S(1)}, f32[64]{0:T(128)}, u32[]{:S(2)}) copy-start(f32[64]{0:T(128)} %get-tuple-element.235) | copy-start | bytes 772
  154.3 12.2 %copy-start.114 = (f32[64]{0:T(128)S(1)}, f32[64]{0:T(128)}, u32[]{:S(2)}) copy-start(f32[64]{0:T(128)} %get-tuple-element.186) | copy-start | bytes 772
  154.3 13.0 %copy-start.24 = (f32[64]{0:T(128)S(1)}, f32[64]{0:T(128)}, u32[]{:S(2)}) copy-start(f32[64]{0:T(128)} %copy-done.23) | copy-start | bytes 772
  154.3 13.0 %copy-start.50 = (f32[64]{0:T(128)S(1)}, f32[64]{0:T(128)}, u32[]{:S(2)}) copy-start(f32[64]{0:T(128)} %get-tuple-element.234) | copy-start | bytes 772
  154.3 13.0 %copy-start.103 = (f32[64]{0:T(128)S(1)}, f32[64]{0:T(128)}, u32[]{:S(2)}) copy-start(f32[64]{0:T(128)} %get-tuple-element.185) | copy-start | bytes 772
  155.1 13.0 %copy-start.42 = (f32[64]{0:T(128)S(1)}, f32[64]{0:T(128)}, u32[]{:S(2)}) copy-start(f32[64]{0:T(128)} %get-tuple-element.233) | copy-start | bytes 772
  155.1 13.0 %copy-start.94 = (f32[64]{0:T(128)S(1)}, f32[64]{0:T(128)}, u32[]{:S(2)}) copy-start(f32[64]{0:T(128)} %get-tuple-element.184) | copy-start | bytes 772
  156.0 13.0 %copy-start.36 = (f32[64]{0:T(128)S(1)}, f32[64]{0:T(128)}, u32[]{:S(2)}) copy-start(f32[64]{0:T(128)} %get-tuple-element.232) | copy-start | bytes 772
  156.0 13.0 %copy-start.84 = (f32[64]{0:T(128)S(1)}, f32[64]{0:T(128)}, u32[]{:S(2)}) copy-start(f32[64]{0:T(128)} %get-tuple-element.183) | copy-start | bytes 772
  156.8 13.1 %copy-start.30 = (f32[64]{0:T(128)S(1)}, f32[64]{0:T(128)}, u32[]{:S(2)}) copy-start(f32[64]{0:T(128)} %get-tuple-element.231) | copy-start | bytes 772
  156.8 13.1 %copy-start.74 = (f32[64]{0:T(128)S(1)}, f32[64]{0:T(128)}, u32[]{:S(2)}) copy-start(f32[64]{0:T(128)} %get-tuple-element.182) | copy-start | bytes 772
  156.8 13.1 %copy-start.128 = (f32[64]{0:T(128)S(1)}, f32[64]{0:T(128)}, u32[]{:S(2)}) copy-start(f32[64]{0:T(128)} %get-tuple-element.134) | copy-start | bytes 772
  157.7 13.1 %copy-start.22 = (f32[64]{0:T(128)S(1)}, f32[64]{0:T(128)}, u32[]{:S(2)}) copy-start(f32[64]{0:T(128)} %get-tuple-element.229) | copy-start | bytes 772
  157.7 13.1 %copy-start.64 = (f32[64]{0:T(128)S(1)}, f32[64]{0:T(128)}, u32[]{:S(2)}) copy-start(f32[64]{0:T(128)} %get-tuple-element.181) | copy-start | bytes 772
  157.7 13.1 %copy-start.118 = (f32[64]{0:T(128)S(1)}, f32[64]{0:T(128)}, u32[]{:S(2)}) copy-start(f32[64]{0:T(128)} %get-tuple-element.133) | copy-start | bytes 772
  158.5 13.2 %copy-start.20 = (f32[64]{0:T(128)S(1)}, f32[64]{0:T(128)}, u32[]{:S(2)}) copy-start(f32[64]{0:T(128)} %get-tuple-element.228) | copy-start | bytes 772
  158.5 13.2 %copy-start.54 = (f32[64]{0:T(128)S(1)}, f32[64]{0:T(128)}, u32[]{:S(2)}) copy-start(f32[64]{0:T(128)} %get-tuple-element.180) | copy-start | bytes 772
  158.5 13.2 %copy-start.107 = (f32[64]{0:T(128)S(1)}, f32[64]{0:T(128)}, u32[]{:S(2)}) copy-start(f32[64]{0:T(128)} %get-tuple-element.132) | copy-start | bytes 772
  159.3 12.5 %copy-start.18 = (f32[64]{0:T(128)S(1)}, f32[64]{0:T(128)}, u32[]{:S(2)}) copy-start(f32[64]{0:T(128)} %get-tuple-element.227) | copy-start | bytes 772
  159.3 12.5 %copy-start.44 = (f32[64]{0:T(128)S(1)}, f32[64]{0:T(128)}, u32[]{:S(2)}) copy-start(f32[64]{0:T(128)} %get-tuple-element.179) | copy-start | bytes 772
  159.3 12.5 %copy-start.96 = (f32[64]{0:T(128)S(1)}, f32[64]{0:T(128)}, u32[]{:S(2)}) copy-start(f32[64]{0:T(128)} %get-tuple-element.131) | copy-start | bytes 772
  159.3 12.5 %copy-start.142 = (f32[64]{0:T(128)S(1)}, f32[64]{0:T(128)}, u32[]{:S(2)}) copy-start(f32[64]{0:T(128)} %get-tuple-element.86) | copy-start | bytes 772
  166.5 11.9 %copy-start.231 = (f32[64]{0:T(128)S(1)}, f32[64]{0:T(128)}, u32[]{:S(2)}) copy-start(f32[64]{0:T(128)} %get-tuple-element.170) | copy-start | bytes 772
  (239 other events, 1281.0 us)
where the time goes:
time: 240 us; the launch traced here: 238 us
  local copies, waits for them, and re-layouts  85.1 us (35%)
  other arithmetic  73.1 us (30%)
  starting transfers between devices  30.3 us (13%)
  blocking collectives  27.3 us (11%)
  matrix products  8.93 us (4%)
  waiting for transfers between devices  7.63 us (3%)
  between operations  5.7 us (2%)
    unnamed x70, other arithmetic  48.4 us
    unnamed x583, local copies, waits for them, and re-layouts  33.3 us
    all_to_all x1, blocking collectives, body(): lax.all_to_all(projected.reshape(owners, span_chan, coeffs, atom_count),...  27.3 us
    all_to_all x1, starting transfers between devices, body(): lax.all_to_all(outgoing, 'graph', split_axis=2, concat_axis=2, tiled=True)  15.5 us
    slice x8, local copies, waits for them, and re-layouts, body(): weight = weight_full[degree].astype(jnp.bfloat16)  10.9 us
    mul x13, local copies, waits for them, and re-layouts, rotate(): wig_rows[first_row + position * span_cols + column][None, :]  8.54 us
    convert_element_type x2, local copies, waits for them, and re-layouts, body(): source = source.astype(jnp.float32)  8.33 us
    gather x1, local copies, waits for them, and re-layouts, body(): lookup[:, :, edge_source]  7.66 us
  transfers between devices with their start and end apart: 3, of which 1 were waited for; matrix products, arithmetic and copies ran while one was open for 20% of the time, Pallas kernels for 0%

commit v1 on v0

--- a/solution.py
+++ b/solution.py
@@ -190,7 +190,9 @@
     per_owner = edge_source.shape[0] // owners
     first_edge = quarter * per_owner
     outgoing = node_feats[:, :, send_list]
-    arrived = lax.all_to_all(outgoing, "graph", split_axis=2, concat_axis=2, tiled=True)
+    cells = jnp.split(outgoing, lax.axis_size("graph"), axis=2)
+    got = lax.all_to_all(jnp.stack(cells), "graph", 0, 0)
+    arrived = jnp.concatenate(got, axis=2)
     packed = jnp.concatenate(
         [norm_gain, project_weight.astype(jnp.float32).reshape(levels, -1)], axis=1
     )

time: 240 us -> 239 us (level)
  other arithmetic: 73.1 us -> 69.4 us
    convert_element_type x0 -> x1, other arithmetic: none -> 3.9 us  [body(): source = source.astype(jnp.float32)]
    unnamed x70, other arithmetic: 48.4 us -> 44.7 us
    unnamed x583 -> x619, local copies, waits for them, and re-layouts: 33.3 us -> 33.9 us
  transfers between devices with their start and end apart: 3 -> 3, of which waited for: 1 -> 1; matrix products, arithmetic and copies ran while one was open for 20% -> 21% of each run, Pallas kernels for 0% -> 0%
where the time goes in v1:
time: 239 us; the launch traced here: 237 us
  local copies, waits for them, and re-layouts  86.6 us (36%)
  other arithmetic  69.4 us (29%)
  starting transfers between devices  30.3 us (13%)
  blocking collectives  27.1 us (11%)
  matrix products  10.2 us (4%)
  waiting for transfers between devices  7.06 us (3%)
  between operations  5.95 us (2%)
    unnamed x70, other arithmetic  44.7 us
    unnamed x619, local copies, waits for them, and re-layouts  33.9 us
    all_to_all x1, blocking collectives, body(): lax.all_to_all(projected.reshape(owners, span_chan, coeffs, atom_count),...  27.1 us
    all_to_all x1, starting transfers between devices, body(): got = lax.all_to_all(jnp.stack(cells), 'graph', 0, 0)  15.5 us
    slice x8, local copies, waits for them, and re-layouts, body(): weight = weight_full[degree].astype(jnp.bfloat16)  11.7 us
    mul x13, local copies, waits for them, and re-layouts, rotate(): wig_rows[first_row + position * span_cols + column][None, :]  8.58 us
    convert_element_type x2, local copies, waits for them, and re-layouts, body(): source = source.astype(jnp.float32)  8.37 us
    gather x1, local copies, waits for them, and re-layouts, body(): lookup[:, :, edge_source]  7.55 us
  transfers between devices with their start and end apart: 3, of which 1 were waited for; matrix products, arithmetic and copies ran while one was open for 21% of the time, Pallas kernels for 0%

profile of v1, /device:TPU:2, one launch (start us, length us, event | category | flops | bytes accessed | tf_op | source)
XLA Modules:
  0.0 236.7 jit_solution(15608196894159535433)
XLA Ops:
  0.0 1.2 copy.235
  3.8 2.0 reshape.3043
  5.8 15.5 %all-to-all-start.1 = ((bf16[32,2,1568]{2,1,0:T(2,128)(2,1)}), bf16[32,2,1568]{2,1,0:T(2,128)(2,1)S(1)}, u32[]{:S(2)}, u32[]{:S(2)}) async-start(bf16[32,2,1568]{2,1,0:T(2,128)(2,1)} %reshape.3043), calls=%async_computation.1 | async-start | bytes 425984 | tf_op jit(solution)/shard_map/all_to_all | solution.py:194
  21.3 0.9 dynamic-slice_convert_fusion
  30.2 1.2 compare_select_fusion.2
  34.0 0.9 fusion.26
  35.0 7.1 %all-to-all-done.1 = bf16[32,2,1568]{2,1,0:T(2,128)(2,1)S(1)} async-done(((bf16[32,2,1568]{2,1,0:T(2,128)(2,1)}), bf16[32,2,1568]{2,1,0:T(2,128)(2,1)S(1)}, u32[]{:S(2)}, u32[]{:S(2)}) %all-to-all-start.1) | async-done | bytes 200736 | tf_op jit(solution)/shard_map/all_to_all | solution.py:194
  42.0 0.9 broadcast_in_dim.56
  42.9 7.5 %all-to-all-start = ((f32[16,7,1032]{2,1,0:T(8,128)}), f32[16,7,1032]{2,1,0:T(8,128)S(1)}, u32[]{:S(2)}, u32[]{:S(2)}) async-start(f32[16,7,1032]{2,1,0:T(8,128)} %broadcast_in_dim.56), calls=%async_computation | async-start | bytes 1179648 | tf_op jit(solution)/shard_map/all_to_all | solution.py:199
  50.4 2.5 %reshape.3044 = bf16[32,8,8,49]{3,2,1,0:T(8,128)(2,1)S(1)} reshape(bf16[32,2,1568]{2,1,0:T(2,128)(2,1)} %copy-done.10) | data formatting | bytes 401408
  53.0 7.5 %gather_fusion.1 = bf16[1024,49,8]{1,2,0:T(8,128)(2,1)} fusion(bf16[49,8,320]{0,1,2:T(8,128)(2,1)S(1)} %pad_maximum_fusion, s32[1024]{0:T(1024)S(1)} %get-tuple-element.263), kind=kCustom, calls=%fused_computation.1 | custom fusion | bytes 1609728 | tf_op jit(solution)/shard_map/gather | solution.py:210
  60.6 3.1 %bitcast_bitcast_fusion = bf16[1024,8,49]{2,1,0:T(8,128)(2,1)} fusion(bf16[1024,49,8]{1,2,0:T(8,128)(2,1)} %gather_fusion.1), kind=kLoop, calls=%fused_computation.555 | loop fusion | bytes 1605632
  63.7 5.8 %reshape.3045 = bf16[16,2,12544]{2,1,0:T(2,128)(2,1)} reshape(bf16[1024,8,49]{2,1,0:T(8,128)(2,1)} %bitcast_bitcast_fusion) | data formatting | bytes 1605632
  69.5 7.4 %all-to-all-start.2 = ((bf16[16,2,12544]{2,1,0:T(2,128)(2,1)}), bf16[16,2,12544]{2,1,0:T(2,128)(2,1)}, u32[]{:S(2)}, u32[]{:S(2)}) async-start(bf16[16,2,12544]{2,1,0:T(2,128)(2,1)} %reshape.3045), calls=%async_computation.2 | async-start | bytes 1605632 | tf_op jit(solution)/shard_map/all_to_all | solution.py:209
  79.6 1.8 copy.231
  81.5 1.3 fusion.73
  82.7 1.8 copy.276
  84.6 1.7 copy.272
  86.3 1.8 copy.268
  88.1 1.8 copy.264
  89.8 1.7 copy.260
  93.7 7.8 %reshape.3046 = bf16[1024,8,49]{2,1,0:T(8,128)(2,1)} reshape(bf16[16,2,12544]{2,1,0:T(2,128)(2,1)} %all-to-all-done.2) | data formatting | bytes 1605632
  101.5 3.1 %multiply_reduce_fusion = f32[49,1024]{0,1:T(8,128)S(1)} fusion(bf16[1024,8,49]{2,1,0:T(8,128)(2,1)} %reshape.3046), kind=kLoop, calls=%fused_computation.6 | loop fusion | flops 1154048 | bytes 1003520 | tf_op jit(solution)/shard_map/reduce_sum | solution.py:213
  105.7 3.9 %bitcast_convert_fusion.3 = f32[49,8,1024]{0,1,2:T(8,128)} fusion(bf16[1024,8,49]{2,1,0:T(8,128)(2,1)} %reshape.3046), kind=kLoop, calls=%fused_computation.554 | loop fusion | flops 401408 | bytes 2408448 | tf_op jit(solution)/shard_map/convert_element_type | solution.py:212
  110.4 5.6 %copy.238 = f32[49,16,8,64]{3,2,1,0:T(8,128)} copy(f32[49,16,8,64]{0,2,3,1:T(8,128)} %bitcast.875) | data formatting | bytes 3211264 | tf_op jit(solution)/shard_map/convert_element_type | solution.py:212
  116.0 2.8 %copy.240 = f32[49,128,64]{1,2,0:T(8,128)S(1)} copy(f32[49,128,64]{2,1,0:T(8,128)} %bitcast.876) | data formatting | bytes 3211264 | tf_op jit(solution)/shard_map/convert_element_type | solution.py:212
  120.6 1.4 constant_dynamic-update-slice_fusion.61
  122.0 1.6 constant_dynamic-update-slice_fusion.57
  125.6 0.9 constant_dynamic-update-slice_fusion.53
  132.0 1.0 constant_dynamic-update-slice_fusion.39
  133.1 1.4 constant_dynamic-update-slice_fusion.50
  141.4 1.4 fusion.9
  181.6 1.1 copy.275
  183.3 1.1 copy.271
  184.8 1.0 copy.267
  186.3 0.9 fusion.52
  187.2 1.0 fusion.54
  189.1 0.9 fusion.57
  189.9 0.9 convolution_add_fusion.1
  191.0 1.0 constant_dynamic-update-slice_fusion.119
  192.0 1.1 bitcast_dynamic-update-slice_fusion.3
  193.1 1.1 bitcast_dynamic-update-slice_fusion.2
  194.3 1.9 copy.337
  196.2 3.5 %reshape.3047 = f32[16,1,25088]{2,1,0:T(1,128)S(1)} reshape(f32[16,49,8,64]{3,2,1,0:T(8,128)} %bitcast.877) | data formatting | bytes 3211264
  199.8 27.1 %all_to_all.24 = f32[16,1,25088]{2,1,0:T(1,128)S(1)} all-to-all(f32[16,1,25088]{2,1,0:T(1,128)S(1)} %reshape.3047), channel_id=1, replica_groups=mesh['graph'=32,'irreps'=16] {'irreps'}, dimensions={0} | all-to-all | bytes 3211264 | tf_op jit(solution)/shard_map/all_to_all | solution.py:249
  227.4 4.5 %reduce.4 = f32[16,25088]{1,0:T(8,128)S(1)} reduce(f32[16,1,25088]{2,1,0:T(1,128)S(1)} %all_to_all.24, f32[]{:T(128)} %broadcast.1939), dimensions={1}, to_apply=%all_to_all.19.reduce_sub_computation | reduce | bytes 3211268 | tf_op jit(solution)/shard_map/all_to_all | solution.py:249
  231.9 2.0 reshape.3048
  233.9 2.2 bitcast_reduce_fusion
  (780 shorter events, 73.4 us)
Async XLA Ops:
  0.0 141.4 %copy-start = (bf16[896,896]{1,0:T(8,128)(2,1)S(1)}, bf16[896,896]{1,0:T(8,128)(2,1)}, u32[]{:S(2)}) copy-start(bf16[896,896]{1,0:T(8,128)(2,1)} %param.32) | copy-start | bytes 4816900
  0.0 31.4 %copy-start.20 = (bf16[7,128,8]{1,2,0:T(8,128)(2,1)S(1)}, bf16[7,128,8]{1,2,0:T(8,128)(2,1)}, u32[]{:S(2)}) copy-start(bf16[7,128,8]{1,2,0:T(8,128)(2,1)} %param.35) | copy-start | bytes 43012
  3.5 29.7 %copy-start.276 = (s32[1024]{0:T(1024)S(1)}, s32[1024]{0:T(1024)}, u32[]{:S(2)}) copy-start(s32[1024]{0:T(1024)} %param.24) | copy-start | bytes 12292
  3.5 30.4 %copy-start.277 = (f32[7,8]{1,0:T(8,128)S(1)}, f32[7,8]{1,0:T(8,128)}, u32[]{:S(2)}) copy-start(f32[7,8]{1,0:T(8,128)} %param.21) | copy-start | bytes 676
  3.6 30.4 %copy-start.280 = (bf16[512,128]{1,0:T(8,128)(2,1)S(1)}, bf16[512,128]{1,0:T(8,128)(2,1)}, u32[]{:S(2)}) copy-start(bf16[512,128]{1,0:T(8,128)(2,1)} %param.29) | copy-start | bytes 393220
  5.8 36.2 %all-to-all-start.1 = ((bf16[32,2,1568]{2,1,0:T(2,128)(2,1)}), bf16[32,2,1568]{2,1,0:T(2,128)(2,1)S(1)}, u32[]{:S(2)}, u32[]{:S(2)}) async-start(bf16[32,2,1568]{2,1,0:T(2,128)(2,1)} %reshape.3043), calls=%async_computation.1 | async-start | bytes 425984 | tf_op jit(solution)/shard_map/all_to_all | solution.py:194
  42.9 26.6 %all-to-all-start = ((f32[16,7,1032]{2,1,0:T(8,128)}), f32[16,7,1032]{2,1,0:T(8,128)S(1)}, u32[]{:S(2)}, u32[]{:S(2)}) async-start(f32[16,7,1032]{2,1,0:T(8,128)} %broadcast_in_dim.56), calls=%async_computation | async-start | bytes 1179648 | tf_op jit(solution)/shard_map/all_to_all | solution.py:199
  63.7 13.8 %copy-start.2 = (s32[64]{0:T(128)S(1)}, s32[64]{0:T(128)}, u32[]{:S(2)}) copy-start(s32[64]{0:T(128)} %param.22) | copy-start | bytes 772
  69.5 24.2 %all-to-all-start.2 = ((bf16[16,2,12544]{2,1,0:T(2,128)(2,1)}), bf16[16,2,12544]{2,1,0:T(2,128)(2,1)}, u32[]{:S(2)}, u32[]{:S(2)}) async-start(bf16[16,2,12544]{2,1,0:T(2,128)(2,1)} %reshape.3045), calls=%async_computation.2 | async-start | bytes 1605632 | tf_op jit(solution)/shard_map/all_to_all | solution.py:209
  143.6 11.0 %copy-start.69 = (f32[64]{0:T(128)S(1)}, f32[64]{0:T(128)}, u32[]{:S(2)}) copy-start(f32[64]{0:T(128)} %get-tuple-element.60) | copy-start | bytes 772
  143.6 11.8 %copy-start.63 = (f32[64]{0:T(128)S(1)}, f32[64]{0:T(128)}, u32[]{:S(2)}) copy-start(f32[64]{0:T(128)} %get-tuple-element.59) | copy-start | bytes 772
  143.7 12.5 %copy-start.59 = (f32[64]{0:T(128)S(1)}, f32[64]{0:T(128)}, u32[]{:S(2)}) copy-start(f32[64]{0:T(128)} %get-tuple-element.58) | copy-start | bytes 772
  143.8 13.3 %copy-start.55 = (f32[64]{0:T(128)S(1)}, f32[64]{0:T(128)}, u32[]{:S(2)}) copy-start(f32[64]{0:T(128)} %get-tuple-element.57) | copy-start | bytes 772
  144.7 13.2 %copy-start.51 = (f32[64]{0:T(128)S(1)}, f32[64]{0:T(128)}, u32[]{:S(2)}) copy-start(f32[64]{0:T(128)} %get-tuple-element.56) | copy-start | bytes 772
  145.6 13.2 %copy-start.47 = (f32[64]{0:T(128)S(1)}, f32[64]{0:T(128)}, u32[]{:S(2)}) copy-start(f32[64]{0:T(128)} %get-tuple-element.55) | copy-start | bytes 772
  146.4 13.1 %copy-start.43 = (f32[64]{0:T(128)S(1)}, f32[64]{0:T(128)}, u32[]{:S(2)}) copy-start(f32[64]{0:T(128)} %get-tuple-element.54) | copy-start | bytes 772
  147.2 13.1 %copy-start.39 = (f32[64]{0:T(128)S(1)}, f32[64]{0:T(128)}, u32[]{:S(2)}) copy-start(f32[64]{0:T(128)} %get-tuple-element.53) | copy-start | bytes 772
  147.2 13.1 %copy-start.97 = (f32[64]{0:T(128)S(1)}, f32[64]{0:T(128)}, u32[]{:S(2)}) copy-start(f32[64]{0:T(128)} %get-tuple-element.98) | copy-start | bytes 772
  148.0 13.2 %copy-start.35 = (f32[64]{0:T(128)S(1)}, f32[64]{0:T(128)}, u32[]{:S(2)}) copy-start(f32[64]{0:T(128)} %get-tuple-element.52) | copy-start | bytes 772
  148.0 13.2 %copy-start.89 = (f32[64]{0:T(128)S(1)}, f32[64]{0:T(128)}, u32[]{:S(2)}) copy-start(f32[64]{0:T(128)} %get-tuple-element.97) | copy-start | bytes 772
  148.8 13.2 %copy-start.33 = (f32[64]{0:T(128)S(1)}, f32[64]{0:T(128)}, u32[]{:S(2)}) copy-start(f32[64]{0:T(128)} %get-tuple-element.47) | copy-start | bytes 772
  148.8 13.2 %copy-start.83 = (f32[64]{0:T(128)S(1)}, f32[64]{0:T(128)}, u32[]{:S(2)}) copy-start(f32[64]{0:T(128)} %get-tuple-element.96) | copy-start | bytes 772
  149.6 13.2 %copy-start.31 = (f32[64]{0:T(128)S(1)}, f32[64]{0:T(128)}, u32[]{:S(2)}) copy-start(f32[64]{0:T(128)} %get-tuple-element.51) | copy-start | bytes 772
  149.6 13.2 %copy-start.77 = (f32[64]{0:T(128)S(1)}, f32[64]{0:T(128)}, u32[]{:S(2)}) copy-start(f32[64]{0:T(128)} %get-tuple-element.95) | copy-start | bytes 772
  150.4 13.1 %copy-start.29 = (f32[64]{0:T(128)S(1)}, f32[64]{0:T(128)}, u32[]{:S(2)}) copy-start(f32[64]{0:T(128)} %get-tuple-element.50) | copy-start | bytes 772
  150.5 13.1 %copy-start.71 = (f32[64]{0:T(128)S(1)}, f32[64]{0:T(128)}, u32[]{:S(2)}) copy-start(f32[64]{0:T(128)} %get-tuple-element.94) | copy-start | bytes 772
  151.3 13.1 %copy-start.25 = (f32[64]{0:T(128)S(1)}, f32[64]{0:T(128)}, u32[]{:S(2)}) copy-start(f32[64]{0:T(128)} %get-tuple-element.49) | copy-start | bytes 772
  151.3 13.1 %copy-start.65 = (f32[64]{0:T(128)S(1)}, f32[64]{0:T(128)}, u32[]{:S(2)}) copy-start(f32[64]{0:T(128)} %get-tuple-element.93) | copy-start | bytes 772
  152.1 13.1 %copy-start.61 = (f32[64]{0:T(128)S(1)}, f32[64]{0:T(128)}, u32[]{:S(2)}) copy-start(f32[64]{0:T(128)} %get-tuple-element.92) | copy-start | bytes 772
  152.1 13.1 %copy-start.107 = (f32[64]{0:T(128)S(1)}, f32[64]{0:T(128)}, u32[]{:S(2)}) copy-start(f32[64]{0:T(128)} %get-tuple-element.138) | copy-start | bytes 772
  152.9 13.2 %copy-start.27 = (f32[64]{0:T(128)S(1)}, f32[64]{0:T(128)}, u32[]{:S(2)}) copy-start(f32[64]{0:T(128)} %get-tuple-element.46) | copy-start | bytes 772
  152.9 13.2 %copy-start.57 = (f32[64]{0:T(128)S(1)}, f32[64]{0:T(128)}, u32[]{:S(2)}) copy-start(f32[64]{0:T(128)} %get-tuple-element.91) | copy-start | bytes 772
  152.9 13.2 %copy-start.99 = (f32[64]{0:T(128)S(1)}, f32[64]{0:T(128)}, u32[]{:S(2)}) copy-start(f32[64]{0:T(128)} %get-tuple-element.137) | copy-start | bytes 772
  153.7 10.6 %copy-start.113 = (f32[64]{0:T(128)S(1)}, f32[64]{0:T(128)}, u32[]{:S(2)}) copy-start(f32[64]{0:T(128)} %get-tuple-element.139) | copy-start | bytes 772
  153.7 13.1 %copy-start.23 = (f32[64]{0:T(128)S(1)}, f32[64]{0:T(128)}, u32[]{:S(2)}) copy-start(f32[64]{0:T(128)} %get-tuple-element.45) | copy-start | bytes 772
  153.7 13.1 %copy-start.53 = (f32[64]{0:T(128)S(1)}, f32[64]{0:T(128)}, u32[]{:S(2)}) copy-start(f32[64]{0:T(128)} %get-tuple-element.90) | copy-start | bytes 772
  153.8 13.1 %copy-start.91 = (f32[64]{0:T(128)S(1)}, f32[64]{0:T(128)}, u32[]{:S(2)}) copy-start(f32[64]{0:T(128)} %get-tuple-element.136) | copy-start | bytes 772
  154.6 13.1 %copy-start.49 = (f32[64]{0:T(128)S(1)}, f32[64]{0:T(128)}, u32[]{:S(2)}) copy-start(f32[64]{0:T(128)} %get-tuple-element.89) | copy-start | bytes 772
  154.6 13.1 %copy-start.85 = (f32[64]{0:T(128)S(1)}, f32[64]{0:T(128)}, u32[]{:S(2)}) copy-start(f32[64]{0:T(128)} %get-tuple-element.134) | copy-start | bytes 772
  155.4 12.5 %copy-start.45 = (f32[64]{0:T(128)S(1)}, f32[64]{0:T(128)}, u32[]{:S(2)}) copy-start(f32[64]{0:T(128)} %get-tuple-element.88) | copy-start | bytes 772
  155.4 12.5 %copy-start.79 = (f32[64]{0:T(128)S(1)}, f32[64]{0:T(128)}, u32[]{:S(2)}) copy-start(f32[64]{0:T(128)} %get-tuple-element.133) | copy-start | bytes 772
  156.2 11.7 %copy-start.126 = (f32[64]{0:T(128)S(1)}, f32[64]{0:T(128)}, u32[]{:S(2)}) copy-start(f32[64]{0:T(128)} %get-tuple-element.181) | copy-start | bytes 772
  156.3 11.8 %copy-start.41 = (f32[64]{0:T(128)S(1)}, f32[64]{0:T(128)}, u32[]{:S(2)}) copy-start(f32[64]{0:T(128)} %get-tuple-element.87) | copy-start | bytes 772
  156.3 11.8 %copy-start.73 = (f32[64]{0:T(128)S(1)}, f32[64]{0:T(128)}, u32[]{:S(2)}) copy-start(f32[64]{0:T(128)} %get-tuple-element.132) | copy-start | bytes 772
  156.3 11.8 %copy-start.117 = (f32[64]{0:T(128)S(1)}, f32[64]{0:T(128)}, u32[]{:S(2)}) copy-start(f32[64]{0:T(128)} %get-tuple-element.180) | copy-start | bytes 772
  157.1 11.2 %copy-start.37 = (f32[64]{0:T(128)S(1)}, f32[64]{0:T(128)}, u32[]{:S(2)}) copy-start(f32[64]{0:T(128)} %get-tuple-element.86) | copy-start | bytes 772
  157.1 11.2 %copy-start.67 = (f32[64]{0:T(128)S(1)}, f32[64]{0:T(128)}, u32[]{:S(2)}) copy-start(f32[64]{0:T(128)} %get-tuple-element.131) | copy-start | bytes 772
  157.1 11.2 %copy-start.111 = (f32[64]{0:T(128)S(1)}, f32[64]{0:T(128)}, u32[]{:S(2)}) copy-start(f32[64]{0:T(128)} %get-tuple-element.179) | copy-start | bytes 772
  (243 other events, 1209.5 us)
